TPU v7x, 32 devices: a whole 2x2x4 slice. The times are simulated.
32 devices in a mesh: chain: 8 (over z, x), grp: 4 (over y, core).
Axes of the slice: x: 2, y: 2, z: 4, core: 2. Of those that a mesh axis runs over, the one named last changes fastest.
Arguments:
- right_side: float32 [16, 4, 64, 128], P('chain', 'grp'), may hold values from -0.8 to 0.8
- factor: float32 [16, 4, 2, 128, 128], P('chain', 'grp'), may hold values from -1 to 1
- inverse_diag: float32 [16, 4, 128, 128], P('chain', 'grp'), as said below
- pattern: int32 [16, 4, 2], P('chain'), may hold values from 0 to 3, as said below
Outputs:
- forward_result: float32 [16, 4, 64, 128], P('chain', 'grp')
- solution: float32 [16, 4, 64, 128], P('chain', 'grp')
Inputs may be any that keep to these rules, and one draw needn't show every extreme that they name: `pattern`: the 2 entries of one supernode are different supernodes of the previous level. `inverse_diag`: every block is lower triangular with a diagonal between 0.75 and 1.05.
All inputs are finite; a program needn't handle non-finite values.
Results may differ from a plain program's by a relative error of at most 0.0002.
Values sent between devices are 32-bit elements; how exact they have to be, the bound alone decides.
No kernel may reach another device: no remote copies, remote signals or barrier semaphores. Data moves between devices by JAX's collectives and lax.ppermute only.
A program may use at most 320 MiB of HBM per device.

v0:
```python
import jax
import jax.numpy as jnp
from jax import lax
from jax.sharding import PartitionSpec as P

PRECISE = lax.Precision.HIGHEST


def carried_in(value, axis, join, neutral, backward):
    count, mine = (lax.axis_size(axis), lax.axis_index(axis))
    pieces = jax.tree.map(lambda part: lax.all_gather(part, axis), value)
    if backward:
        pieces = jax.tree.map(lambda part: part[::-1], pieces)
        mine = count - 1 - mine
    subtotal = jax.tree.map(
        lambda part, zero: jnp.full_like(part, 0) + jnp.asarray(zero, part.dtype), value, neutral
    )

    def hop(position, subtotal):
        longer = join(subtotal, jax.tree.map(lambda part: part[position], pieces))
        return jax.tree.map(lambda new, old: jnp.where(position < mine, new, old), longer, subtotal)

    return lax.fori_loop(0, count - 1, hop, subtotal)


def matmul(left_side, right_factor):
    return jnp.dot(left_side, right_factor, precision=PRECISE, preferred_element_type=jnp.float32)


def matmul_trans(left_side, right_factor):
    return lax.dot_general(
        left_side,
        right_factor,
        (((1,), (1,)), ((), ())),
        precision=PRECISE,
        preferred_element_type=jnp.float32,
    )


def combine_forward(earlier_map, later_map):
    return (
        matmul(earlier_map[0], later_map[0]),
        matmul(earlier_map[1], later_map[0]) + later_map[1],
    )


def combine_backward(earlier_map, later_map):
    return (
        matmul(later_map[0], earlier_map[0]),
        matmul_trans(earlier_map[1], later_map[0]) + later_map[1],
    )


def fold_maps(running, inputs):
    return ((matmul(running[0], inputs[0]), matmul(running[1], inputs[0]) + inputs[1]), None)


def forward_step(previous, inputs):
    updated = matmul(previous, inputs[0]) + inputs[1]
    return (updated, updated)


def back_fold(running, inputs):
    return (matmul_trans(running - inputs[1], inputs[0]), None)


def shards(right_side, factor, inverse_diag, pattern):
    levels = right_side.shape[0]
    samples = right_side.shape[2]
    sup_rows = right_side.shape[3]
    groups = lax.axis_size("grp")
    level_rows = groups * sup_rows
    my_group = lax.axis_index("grp")
    scaled = jnp.einsum(
        "lgti,lgkij->lgktj",
        inverse_diag,
        factor,
        precision=PRECISE,
        preferred_element_type=jnp.float32,
    )
    lifted = jnp.einsum(
        "lgsi,lgti->lgst",
        right_side,
        inverse_diag,
        precision=PRECISE,
        preferred_element_type=jnp.float32,
    )
    blocks, offsets = (
        lax.all_gather(scaled, "grp", axis=1, tiled=True),
        lax.all_gather(lifted, "grp", axis=1, tiled=True),
    )
    onehot = (pattern[..., None] == jnp.arange(groups, dtype=jnp.int32)).astype(jnp.float32)
    level_maps = -jnp.einsum(
        "lgkh,lgktj->lhjgt", onehot, blocks, precision=PRECISE, preferred_element_type=jnp.float32
    )
    level_maps = level_maps.reshape(levels, level_rows, level_rows)
    sources = offsets.transpose(0, 2, 1, 3).reshape(levels, samples, level_rows)
    (total_map, total_shift), _ = lax.scan(
        fold_maps, (level_maps[0], sources[0]), (level_maps[1:], sources[1:])
    )
    neutral = (
        jnp.eye(level_rows, dtype=jnp.float32),
        jnp.zeros((samples, level_rows), jnp.float32),
    )
    _, incoming = carried_in((total_map, total_shift), "chain", combine_forward, neutral, False)
    _, solved = lax.scan(forward_step, incoming, (level_maps, sources))
    forward_own = lax.dynamic_slice_in_dim(solved, my_group * sup_rows, sup_rows, 2)
    back_shift, _ = lax.scan(
        back_fold, jnp.zeros((samples, level_rows), jnp.float32), (level_maps, solved), reverse=True
    )
    _, arriving = carried_in((total_map, back_shift), "chain", combine_backward, neutral, True)
    own_inverse = inverse_diag[:, 0]

    def back_step(running, inputs):
        level_map, forward_rows, inverse = inputs
        own_rows = lax.dynamic_slice_in_dim(forward_rows, my_group * sup_rows, sup_rows, 1)
        own_pending = lax.dynamic_slice_in_dim(running, my_group * sup_rows, sup_rows, 1)
        answer = matmul(own_rows - own_pending, inverse)
        return (matmul_trans(running - forward_rows, level_map), answer)

    _, answers = lax.scan(back_step, arriving, (level_maps, solved, own_inverse), reverse=True)
    return (forward_own[:, None], answers[:, None])


def solution(mesh):
    return jax.shard_map(
        shards,
        mesh=mesh,
        in_specs=(
            P("chain", "grp", None, None),
            P("chain", "grp", None, None, None),
            P("chain", "grp", None, None),
            P("chain", None, None),
        ),
        out_specs=(P("chain", "grp", None, None), P("chain", "grp", None, None)),
        check_vma=False,
    )
```

profile of v0, /device:TPU:0, one launch (start us, length us, event | category | flops | bytes accessed | tf_op | source)
XLA Modules:
  0.0 289.6 jit_solution(16148861564298682824)
XLA Ops:
  12.6 7.2 %all-gather.1 = f32[2,256,128]{2,1,0:T(8,128)S(1)} all-gather(f32[2,64,128]{2,1,0:T(8,128)S(1)} %fusion.50), channel_id=3, replica_groups=mesh['chain'=8,'grp'=4] {'grp'}, dimensions={1}, use_global_device_ids=true | all-gather | bytes 327680 | tf_op jit(solution)/shard_map/all_gather | solution.py:90
  20.8 9.2 %all-gather.9.cloned.1.call-done = f32[2,4,2,128,128]{4,3,2,0,1:T(8,128)} async-done(((f32[2,1,2,128,128]{4,3,2,0,1:T(8,128)}), f32[2,4,2,128,128]{4,3,2,0,1:T(8,128)}) %all-gather.9.cloned.1.call-update) | async-done | bytes 1048592 | tf_op jit(solution)/shard_map/all_gather | solution.py:89
  30.1 3.9 %negate_bitcast_fusion = f32[2,4,128,4,128]{2,1,4,3,0:T(4,128)S(1)} fusion(f32[2,4,2,128,128]{4,3,2,0,1:T(8,128)} %all-gather.9.cloned.1.call-done, s32[2,4,2]{2,1,0:T(4,128)S(1)} %copy.23), kind=kOutput, calls=%fused_computation.46 | convolution fusion | flops 13107264 | bytes 3145792 | tf_op jit(solution)/shard_map/lgkh,lgktj->lhjgt/dot_general | solution.py:93
  37.0 5.7 %fusion.39 = f32[512,512]{1,0:T(8,128)} fusion(f32[64,8,4,128]{3,2,1,0:T(4,128)} %bitcast.155, f32[64,8,4,128]{3,2,1,0:T(4,128)S(1)} %bitcast.154), kind=kOutput, calls=%fused_computation.50 | convolution fusion | flops 1610612736 | bytes 3145728 | tf_op jit(solution)/shard_map/while/body/eval_jaxpr/dot_general | solution.py:27
  47.8 29.5 %all-gather.13.cloned.1.call-done = f32[512,512]{1,0:T(8,128)} async-done(((f32[64,512]{1,0:T(8,128)}), f32[512,512]{1,0:T(8,128)}) %all-gather.13.cloned.1.call-update) | async-done | bytes 1048592 | tf_op jit(solution)/shard_map/all_gather | solution.py:11
  77.3 125.4 %all-gather.11.cloned.1.call-done = f32[4096,512]{1,0:T(8,128)} async-done(((f32[512,512]{1,0:T(8,128)}), f32[4096,512]{1,0:T(8,128)}) %all-gather.11.cloned.1.call-update) | async-done | bytes 8388624 | tf_op jit(solution)/shard_map/all_gather | solution.py:11
  202.7 14.4 %while.79 = (s32[]{:T(128)}, f32[64,512]{1,0:T(8,128)S(1)}, s32[]{:T(128)}, f32[8,512,512]{2,1,0:T(8,128)}, f32[8,64,512]{2,1,0:T(8,128)}, /*index=5*/s32[]{:T(128)}, s32[]{:T(128)}) while((s32[]{:T(128)}, f32[64,512]{1,0:T(8,128)S(1)}, s32[]{:T(128)}, f32[8,512,512]{2,1,0:T(8,128)}, f32[8,64,512]{2,1,0:T(8,128)}, ...), condition=%wide.region_1.2_spmd.clone, body=%wide.region_0.1_spmd.clone.sunk | while | flops 201457664 | bytes 1837671 | solution.py:23
  202.7 2.0 fusion.82
  208.9 2.0 fusion.82
  211.0 2.0 fusion.82
  213.0 2.0 fusion.82
  218.8 2.3 while.77
  221.8 7.6 %rev.6 = f32[8,512,512]{2,1,0:T(8,128)} reverse(f32[8,512,512]{2,1,0:T(8,128)} %get-tuple-element.945), dimensions={0} | reverse | bytes 16777216 | tf_op jit(solution)/shard_map/rev | solution.py:13
  230.0 30.4 %all-gather.15.cloned.1.call-done = f32[512,512]{1,0:T(8,128)} async-done(((f32[64,512]{1,0:T(8,128)}), f32[512,512]{1,0:T(8,128)}) %all-gather.15.cloned.1.call-update) | async-done | bytes 1048592 | tf_op jit(solution)/shard_map/all_gather | solution.py:11
  260.4 2.3 rev.7
  262.7 16.8 %while.80 = (s32[]{:T(128)}, f32[64,512]{1,0:T(8,128)S(1)}, s32[]{:T(128)}, f32[8,512,512]{2,1,0:T(8,128)}, f32[8,64,512]{2,1,0:T(8,128)}, /*index=5*/s32[]{:T(128)}, s32[]{:T(128)}) while((s32[]{:T(128)}, f32[64,512]{1,0:T(8,128)S(1)}, s32[]{:T(128)}, f32[8,512,512]{2,1,0:T(8,128)}, f32[8,64,512]{2,1,0:T(8,128)}, ...), condition=%wide.region_7.8_spmd.clone, body=%wide.region_6.7_spmd.clone.sunk | while | flops 201457664 | bytes 1837671 | solution.py:23
  262.7 2.4 fusion.85
  265.2 2.4 fusion.85
  267.6 2.4 fusion.85
  270.0 2.4 fusion.85
  272.4 2.4 fusion.85
  274.8 2.4 fusion.85
  277.2 2.4 fusion.85
  279.6 2.8 while.78
  (69 shorter events, 30.8 us)
Async XLA Ops:
  7.2 1.0 copy-start
  7.2 22.9 %all-gather.9.cloned.1.call-start = ((), (), s32[]{:S(2)}) async-start(), calls=%async_computation | async-start | bytes 1310720 | tf_op jit(solution)/shard_map/all_gather | solution.py:89
  10.5 66.9 %all-gather.13.cloned.1.call-start = ((), (), s32[]{:S(2)}) async-start(), calls=%async_computation.2 | async-start | bytes 1179648 | tf_op jit(solution)/shard_map/all_gather | solution.py:11
  20.0 0.8 copy-start.3
  34.0 1.2 copy-start.4
  36.9 165.8 %all-gather.11.cloned.1.call-start = ((), (), s32[]{:S(2)}) async-start(), calls=%async_computation.1 | async-start | bytes 9437184 | tf_op jit(solution)/shard_map/all_gather | solution.py:11
  42.7 217.7 %all-gather.15.cloned.1.call-start = ((), (), s32[]{:S(2)}) async-start(), calls=%async_computation.3 | async-start | bytes 1179648 | tf_op jit(solution)/shard_map/all_gather | solution.py:11
  221.1 0.6 copy-start.1
  262.7 16.9 %copy-start.2 = (f32[2,1,128,128]{3,2,1,0:T(8,128)S(1)}, f32[2,1,128,128]{3,2,1,0:T(8,128)}, u32[]{:S(2)}) copy-start(f32[2,1,128,128]{3,2,1,0:T(8,128)} %param.16) | copy-start | bytes 393220
  282.4 0.6 copy-start.5
Sparse Core Ops, SparseCore 0:
  10.6 19.4 all-gather.8
  37.0 40.2 all-gather.12
  79.5 123.1 all-gather.10
  221.9 38.4 all-gather.14
where the time goes:
time: 290 us
  waiting for transfers between devices  195 us (67%)
  matrix products  51.5 us (18%)
  local copies, waits for them, and re-layouts  21.4 us (7%)
  between operations  13.9 us (5%)
  blocking collectives  7.25 us (2%)
    all_gather x3, waiting for transfers between devices, carried_in(): pieces = jax.tree.map(lambda part: lax.all_gather(part, axis), value)  185 us
    dot_general x13, matrix products, matmul(): jnp.dot(left_side, right_factor, precision=PRECISE, preferred_element_typ...  23.7 us
    dot_general x11, matrix products, matmul_trans(): lax.dot_general(left_side, right_factor, (((1,), (1,)), ((), ())), precis...  21 us
    rev x2, local copies, waits for them, and re-layouts, carried_in(): pieces = jax.tree.map(lambda part: part[::-1], pieces)  9.88 us
    all_gather x1, waiting for transfers between devices, shards(): lax.all_gather(scaled, 'grp', axis=1, tiled=True)  9.25 us
    all_gather x1, blocking collectives, shards(): lax.all_gather(lifted, 'grp', axis=1, tiled=True)  7.25 us
  transfers between devices with their start and end apart: 4, of which 4 were waited for; matrix products, arithmetic and copies ran while one was open for 8% of the time, Pallas kernels for 0%

commit v1 on v0

--- a/solution.py
+++ b/solution.py
@@ -4,6 +4,41 @@
 from jax.sharding import PartitionSpec as P
 
 PRECISE = lax.Precision.HIGHEST
+
+
+def fit_sizes(buf):
+    wide_out = lax.axis_index("grp")
+    carry_in = lax.axis_size("grp")
+    buffer = []
+    block_last, then, extra = (carry_in, wide_out, buf.shape[1])
+    for dev_i, u in enumerate(buf.shape):
+        buffer.append(u * block_last if dev_i == 1 else u)
+    outer = jnp.zeros(buffer, buf.dtype)
+    b_next = lax.dynamic_update_slice_in_dim(outer, buf, then * extra, axis=1)
+    w = 1
+    prior = front = buf
+    while w < block_last // 2 + 1:
+        views = []
+        dev_i = 0
+        while dev_i < block_last:
+            views.append((dev_i, (dev_i + 1) % block_last))
+            dev_i = dev_i + 1
+        prior = lax.ppermute(prior, "grp", views)
+        b_next = lax.dynamic_update_slice_in_dim(
+            b_next, prior, (then - w) % block_last * extra, axis=1
+        )
+        if 2 * w < block_last:
+            by_rank = []
+            dev_i = 0
+            while dev_i < block_last:
+                by_rank.append((dev_i, (dev_i - 1) % block_last))
+                dev_i = dev_i + 1
+            front = lax.ppermute(front, "grp", by_rank)
+            b_next = lax.dynamic_update_slice_in_dim(
+                b_next, front, (then + w) % block_last * extra, axis=1
+            )
+        w += 1
+    return b_next
 
 
 def carried_in(value, axis, join, neutral, backward):
@@ -85,10 +120,7 @@
         precision=PRECISE,
         preferred_element_type=jnp.float32,
     )
-    blocks, offsets = (
-        lax.all_gather(scaled, "grp", axis=1, tiled=True),
-        lax.all_gather(lifted, "grp", axis=1, tiled=True),
-    )
+    blocks, offsets = (lax.all_gather(scaled, "grp", axis=1, tiled=True), fit_sizes(lifted))
     onehot = (pattern[..., None] == jnp.arange(groups, dtype=jnp.int32)).astype(jnp.float32)
     level_maps = -jnp.einsum(
         "lgkh,lgktj->lhjgt", onehot, blocks, precision=PRECISE, preferred_element_type=jnp.float32

time: 290 us -> 290 us (level)
  blocking collectives: 7.25 us -> 0 us
  local copies, waits for them, and re-layouts: 21.4 us -> 26.7 us
  starting transfers between devices: 0.34 us -> 3.45 us
    all_gather x1 -> x0, blocking collectives: 7.25 us -> none  [shards(): lax.all_gather(lifted, 'grp', axis=1, tiled=True)]
    dynamic_update_slice x0 -> x4, local copies, waits for them, and re-layouts: none -> 5.39 us  [the longest x2 2.7 us: fit_sizes(): lax.dynamic_update_slice_in_dim(b_next, prior, (then - w) % block_last *...]
    ppermute x0 -> x3, starting transfers between devices: none -> 3.11 us  [the longest x1 2.01 us: fit_sizes(): front = lax.ppermute(front, 'grp', by_rank)]
    all_gather x1, waiting for transfers between devices: 9.25 us -> 6.21 us  [shards(): lax.all_gather(scaled, 'grp', axis=1, tiled=True)]
  transfers between devices with their start and end apart: 4 -> 7, of which waited for: 4 -> 5; matrix products, arithmetic and copies ran while one was open for 8% -> 9% of each run, Pallas kernels for 0% -> 0%
where the time goes in v1:
time: 290 us
  waiting for transfers between devices  193 us (67%)
  matrix products  51.5 us (18%)
  local copies, waits for them, and re-layouts  26.7 us (9%)
  between operations  14 us (5%)
  starting transfers between devices  3.45 us (1%)
    all_gather x3, waiting for transfers between devices, carried_in(): pieces = jax.tree.map(lambda part: lax.all_gather(part, axis), value)  185 us
    dot_general x13, matrix products, matmul(): jnp.dot(left_side, right_factor, precision=PRECISE, preferred_element_typ...  23.7 us
    dot_general x11, matrix products, matmul_trans(): lax.dot_general(left_side, right_factor, (((1,), (1,)), ((), ())), precis...  21 us
    rev x2, local copies, waits for them, and re-layouts, carried_in(): pieces = jax.tree.map(lambda part: part[::-1], pieces)  9.88 us
    all_gather x1, waiting for transfers between devices, shards(): lax.all_gather(scaled, 'grp', axis=1, tiled=True)  6.21 us
  transfers between devices with their start and end apart: 7, of which 5 were waited for; matrix products, arithmetic and copies ran while one was open for 9% of the time, Pallas kernels for 0%

profile of v1, /device:TPU:0, one launch (start us, length us, event | category | flops | bytes accessed | tf_op | source)
XLA Modules:
  0.0 289.6 jit_solution(15318879153333158815)
XLA Ops:
  23.9 6.2 %all-gather.8.cloned.1.call-done = f32[2,4,2,128,128]{4,3,2,0,1:T(8,128)} async-done(((f32[2,1,2,128,128]{4,3,2,0,1:T(8,128)}), f32[2,4,2,128,128]{4,3,2,0,1:T(8,128)}) %all-gather.8.cloned.1.call-update) | async-done | bytes 1048592 | tf_op jit(solution)/shard_map/all_gather | solution.py:123
  30.1 3.9 %negate_bitcast_fusion = f32[2,4,128,4,128]{2,1,4,3,0:T(4,128)S(1)} fusion(f32[2,4,2,128,128]{4,3,2,0,1:T(8,128)} %all-gather.8.cloned.1.call-done, s32[2,4,2]{2,1,0:T(4,128)S(1)} %copy.29), kind=kOutput, calls=%fused_computation.46 | convolution fusion | flops 13107264 | bytes 3145792 | tf_op jit(solution)/shard_map/lgkh,lgktj->lhjgt/dot_general | solution.py:125
  37.0 5.7 %fusion.39 = f32[512,512]{1,0:T(8,128)} fusion(f32[64,8,4,128]{3,2,1,0:T(4,128)} %bitcast.158, f32[64,8,4,128]{3,2,1,0:T(4,128)S(1)} %bitcast.157), kind=kOutput, calls=%fused_computation.50 | convolution fusion | flops 1610612736 | bytes 3145728 | tf_op jit(solution)/shard_map/while/body/eval_jaxpr/dot_general | solution.py:62
  47.8 29.5 %all-gather.12.cloned.1.call-done = f32[512,512]{1,0:T(8,128)} async-done(((f32[64,512]{1,0:T(8,128)}), f32[512,512]{1,0:T(8,128)}) %all-gather.12.cloned.1.call-update) | async-done | bytes 1048592 | tf_op jit(solution)/shard_map/all_gather | solution.py:46
  77.4 125.4 %all-gather.10.cloned.1.call-done = f32[4096,512]{1,0:T(8,128)} async-done(((f32[512,512]{1,0:T(8,128)}), f32[4096,512]{1,0:T(8,128)}) %all-gather.10.cloned.1.call-update) | async-done | bytes 8388624 | tf_op jit(solution)/shard_map/all_gather | solution.py:46
  202.7 14.4 %while.79 = (s32[]{:T(128)}, f32[64,512]{1,0:T(8,128)S(1)}, s32[]{:T(128)}, f32[8,512,512]{2,1,0:T(8,128)}, f32[8,64,512]{2,1,0:T(8,128)}, /*index=5*/s32[]{:T(128)}, s32[]{:T(128)}) while((s32[]{:T(128)}, f32[64,512]{1,0:T(8,128)S(1)}, s32[]{:T(128)}, f32[8,512,512]{2,1,0:T(8,128)}, f32[8,64,512]{2,1,0:T(8,128)}, ...), condition=%wide.region_1.2_spmd.clone, body=%wide.region_0.1_spmd.clone.sunk | while | flops 201457664 | bytes 1837671 | solution.py:58
  202.7 2.0 fusion.82
  204.8 2.0 fusion.82
  211.0 2.0 fusion.82
  213.1 2.0 fusion.82
  215.1 2.0 fusion.82
  218.8 2.3 while.77
  221.8 7.6 %rev.6 = f32[8,512,512]{2,1,0:T(8,128)} reverse(f32[8,512,512]{2,1,0:T(8,128)} %get-tuple-element.945), dimensions={0} | reverse | bytes 16777216 | tf_op jit(solution)/shard_map/rev | solution.py:48
  230.1 30.4 %all-gather.14.cloned.1.call-done = f32[512,512]{1,0:T(8,128)} async-done(((f32[64,512]{1,0:T(8,128)}), f32[512,512]{1,0:T(8,128)}) %all-gather.14.cloned.1.call-update) | async-done | bytes 1048592 | tf_op jit(solution)/shard_map/all_gather | solution.py:46
  260.4 2.3 rev.7
  262.7 16.8 %while.80 = (s32[]{:T(128)}, f32[64,512]{1,0:T(8,128)S(1)}, s32[]{:T(128)}, f32[8,512,512]{2,1,0:T(8,128)}, f32[8,64,512]{2,1,0:T(8,128)}, /*index=5*/s32[]{:T(128)}, s32[]{:T(128)}) while((s32[]{:T(128)}, f32[64,512]{1,0:T(8,128)S(1)}, s32[]{:T(128)}, f32[8,512,512]{2,1,0:T(8,128)}, f32[8,64,512]{2,1,0:T(8,128)}, ...), condition=%wide.region_7.8_spmd.clone, body=%wide.region_6.7_spmd.clone.sunk | while | flops 201457664 | bytes 1837671 | solution.py:58
  262.8 2.4 fusion.85
  265.2 2.4 fusion.85
  267.6 2.4 fusion.85
  270.0 2.4 fusion.85
  272.4 2.4 fusion.85
  274.8 2.4 fusion.85
  277.2 2.4 fusion.85
  279.6 2.8 while.78
  (78 shorter events, 39.1 us)
Async XLA Ops:
  7.2 1.0 copy-start
  7.2 22.9 %all-gather.8.cloned.1.call-start = ((), (), s32[]{:S(2)}) async-start(), calls=%async_computation | async-start | bytes 1310720 | tf_op jit(solution)/shard_map/all_gather | solution.py:123
  10.5 66.9 %all-gather.12.cloned.1.call-start = ((), (), s32[]{:S(2)}) async-start(), calls=%async_computation.2 | async-start | bytes 1179648 | tf_op jit(solution)/shard_map/all_gather | solution.py:46
  11.8 4.4 %collective-permute-start = (f32[2,1,64,128]{3,2,0,1:T(8,128)S(1)}, f32[2,1,64,128]{3,2,0,1:T(8,128)S(1)}, u32[]{:S(2)}, u32[]{:S(2)}) collective-permute-start(f32[2,1,64,128]{3,2,0,1:T(8,128)S(1)} %bitcast.166), channel_id=1, source_target_pairs={{0,1},{1,2},{2,3},{3,0},{4,5},{5,6},{6,7},{7,4},{8,9},{9,10},{10,1... | collective-permute-start | bytes 196616 | tf_op jit(solution)/shard_map/ppermute | solution.py:26
  12.4 8.0 %collective-permute-start.1 = (f32[2,1,64,128]{3,2,0,1:T(8,128)S(1)}, f32[2,1,64,128]{3,2,0,1:T(8,128)S(1)}, u32[]{:S(2)}, u32[]{:S(2)}) collective-permute-start(f32[2,1,64,128]{3,2,0,1:T(8,128)S(1)} %bitcast.167), channel_id=1, source_target_pairs={{0,3},{1,0},{2,1},{3,2},{4,7},{5,4},{6,5},{7,6},{8,11},{9,8},{10,9... | collective-permute-start | bytes 196616 | tf_op jit(solution)/shard_map/ppermute | solution.py:36
  16.3 5.5 %collective-permute-start.2 = (f32[2,1,64,128]{3,2,0,1:T(8,128)S(1)}, f32[2,1,64,128]{3,2,0,1:T(8,128)S(1)}, u32[]{:S(2)}, u32[]{:S(2)}) collective-permute-start(f32[2,1,64,128]{3,2,0,1:T(8,128)S(1)} %collective-permute-done), channel_id=1, source_target_pairs={{0,1},{1,2},{2,3},{3,0},{4,5},{5,6},{6,7},{7,4},{8,9},{9,10},{10,1... | collective-permute-start | bytes 196616 | tf_op jit(solution)/shard_map/ppermute | solution.py:26
  23.1 0.8 copy-start.3
  34.0 1.2 copy-start.4
  37.0 165.8 %all-gather.10.cloned.1.call-start = ((), (), s32[]{:S(2)}) async-start(), calls=%async_computation.1 | async-start | bytes 9437184 | tf_op jit(solution)/shard_map/all_gather | solution.py:46
  42.7 217.7 %all-gather.14.cloned.1.call-start = ((), (), s32[]{:S(2)}) async-start(), calls=%async_computation.3 | async-start | bytes 1179648 | tf_op jit(solution)/shard_map/all_gather | solution.py:46
  221.1 0.6 copy-start.1
  262.7 16.9 %copy-start.2 = (f32[2,1,128,128]{3,2,1,0:T(8,128)S(1)}, f32[2,1,128,128]{3,2,1,0:T(8,128)}, u32[]{:S(2)}) copy-start(f32[2,1,128,128]{3,2,1,0:T(8,128)} %param.16) | copy-start | bytes 393220
  282.4 0.6 copy-start.5
Sparse Core Ops, SparseCore 0:
  10.6 19.4 all-gather.7
  37.1 40.2 all-gather.11
  79.5 123.1 all-gather.9
  221.9 38.4 all-gather.13
